TPU v7x, 256 devices: a whole 4x4x8 slice. The times are simulated.
256 devices in a mesh: gx: 32 (over z, x), gy: 8 (over y, core).
Axes of the slice: x: 4, y: 4, z: 8, core: 2. Of those that a mesh axis runs over, the one named last changes fastest.
Arguments:
- hidden_in: bfloat16 [64, 5120], P(None, 'gx'), may hold values from -60 to 60
- norm1_gain: float32 [5120], P('gx'), may hold values from 0.1 to 1.9
- norm1_bias: float32 [5120], P('gx'), may hold values from -4 to 4
- norm2_gain: float32 [5120], P('gx'), may hold values from 0.1 to 1.9
- norm2_bias: float32 [5120], P('gx'), may hold values from -4 to 4
- w_qkv: bfloat16 [5120, 15360], P('gx', 'gy'), may hold values from -0.078125 to 0.078125
- b_qkv: float32 [15360], P('gy'), may hold values from -4 to 4
- w_out: bfloat16 [5120, 5120], P('gy', 'gx'), may hold values from -0.078125 to 0.078125
- b_out: float32 [5120], P('gx'), may hold values from -4 to 4
- w_up: bfloat16 [5120, 20480], P('gx', 'gy'), may hold values from -0.078125 to 0.078125
- b_up: float32 [20480], P('gy'), may hold values from -4 to 4
- w_down: bfloat16 [20480, 5120], P('gy', 'gx'), may hold values from -0.0390625 to 0.0390625
- b_down: float32 [5120], P('gx'), may hold values from -4 to 4
- key_cache: bfloat16 [64, 40, 1024, 128], P('gx', 'gy'), may hold values from -70 to 70
- value_cache: bfloat16 [64, 40, 1024, 128], P('gx', 'gy'), may hold values from -6 to 6
- lengths: int32 [64], replicated, may hold values from 1 to 1024, 32768 in all
- assignment: int32 [64], replicated, may hold values from 0 to 63, each once
Outputs:
- hidden_out: bfloat16 [64, 5120], P(None, 'gx')
- new_keys: bfloat16 [64, 40, 1024, 128], P('gx', 'gy')
- new_values: bfloat16 [64, 40, 1024, 128], P('gx', 'gy')
Inputs may be any that keep to these rules, and one draw needn't show every extreme that they name: `lengths`: each request's length, the largest exactly 1024. `assignment`: a permutation: every slot holds exactly one request.
All inputs are finite; a program needn't handle non-finite values.
Results may differ from a plain program's by a relative error of at most 0.0068.
Values may be sent and summed in bfloat16 or wider, within the bound.
No kernel may reach another device: no remote copies, remote signals or barrier semaphores. Data moves between devices by JAX's collectives and lax.ppermute only.
A program may use at most 64 MiB of HBM per device.

v0:
```python
import jax
import jax.numpy as jnp
from jax import lax
from jax.sharding import PartitionSpec as P

D = 5120
HD = 128
ROT = 32


def rotate(tensor, position):
    half_rot = ROT // 2
    frequency = 10000.0 ** (-2.0 * jnp.arange(half_rot, dtype=jnp.float32) / ROT)
    angle = position.astype(jnp.float32)[:, None, None] * frequency
    cosine = jnp.cos(angle)
    sine = jnp.sin(angle)
    first_half = tensor[..., :half_rot]
    second_half = tensor[..., half_rot:ROT]
    return jnp.concatenate(
        [
            first_half * cosine - second_half * sine,
            second_half * cosine + first_half * sine,
            tensor[..., ROT:],
        ],
        axis=-1,
    )


def block_scores(query, keys, my_len):
    span_len = keys.shape[2]
    scores = jnp.einsum("shd,shpd->shp", query, keys, preferred_element_type=jnp.float32) * HD ** (
        -0.5
    )
    places = lax.iota(jnp.int32, span_len)
    valid = places[None, None, :] < my_len[:, None, None]
    return (jnp.where(valid, scores, -1e30), valid)


def on_device(
    hidden_in,
    norm1_gain,
    norm1_bias,
    norm2_gain,
    norm2_bias,
    w_qkv,
    b_qkv,
    w_out,
    b_out,
    w_up,
    b_up,
    w_down,
    b_down,
    key_cache,
    value_cache,
    lengths,
    assignment,
):
    requests = hidden_in.shape[0]
    rows_dev = key_cache.shape[0]
    heads_dev = key_cache.shape[1]
    wide_in = hidden_in.astype(jnp.float32)
    sum_rows, sum_squares = lax.psum(
        (jnp.sum(wide_in, axis=1), jnp.sum(wide_in * wide_in, axis=1)), "gx"
    )
    row_mean = sum_rows / D
    row_var = sum_squares / D - row_mean * row_mean
    normed = (wide_in - row_mean[:, None]) * lax.rsqrt(row_var + 1e-05)[:, None]
    attn_in = (normed * norm1_gain + norm1_bias).astype(jnp.bfloat16)
    mlp_in = (normed * norm2_gain + norm2_bias).astype(jnp.bfloat16)
    slot_ids = lax.iota(jnp.int32, requests)
    matches = assignment[:, None] == slot_ids[None, :]
    to_request = matches.astype(jnp.float32)
    attn_slot = jnp.dot(
        matches.T.astype(jnp.bfloat16), attn_in, preferred_element_type=jnp.float32
    ).astype(jnp.bfloat16)
    slot_len = jnp.sum(jnp.where(matches, lengths[:, None], 0), axis=0)
    my_len = lax.dynamic_slice_in_dim(slot_len, lax.axis_index("gx") * rows_dev, rows_dev, 0)
    qkv = (
        lax.psum_scatter(
            jnp.dot(attn_slot, w_qkv, preferred_element_type=jnp.float32),
            "gx",
            scatter_dimension=0,
            tiled=True,
        )
        + b_qkv
    )
    qkv = qkv.reshape(rows_dev, heads_dev, 3, HD)
    position = my_len - 1
    query = rotate(qkv[:, :, 0], position).astype(jnp.bfloat16)
    new_key = rotate(qkv[:, :, 1], position).astype(jnp.bfloat16)
    new_value = qkv[:, :, 2].astype(jnp.bfloat16)
    new_keys = key_cache
    new_values = value_cache
    zero_index = jnp.int32(0)
    for local_slot in range(rows_dev):
        slot_index = jnp.int32(local_slot)
        new_keys = lax.dynamic_update_slice(
            new_keys,
            new_key[local_slot][None, :, None, :],
            (slot_index, zero_index, position[local_slot], zero_index),
        )
        new_values = lax.dynamic_update_slice(
            new_values,
            new_value[local_slot][None, :, None, :],
            (slot_index, zero_index, position[local_slot], zero_index),
        )
    scores, valid = block_scores(query, new_keys, my_len)
    top_score = jnp.max(scores, axis=2)
    weights = jnp.where(valid, jnp.exp(scores - top_score[:, :, None]), 0.0)
    total = jnp.sum(weights, axis=2)
    weights_low = weights.astype(jnp.bfloat16)
    weighted = jnp.einsum(
        "shp,shpd->shd", weights_low, new_values, preferred_element_type=jnp.float32
    )
    attended = (weighted / total[:, :, None]).astype(jnp.bfloat16).reshape(rows_dev, heads_dev * HD)
    slot_part = jnp.dot(
        lax.all_gather(attended, "gx", axis=0, tiled=True),
        w_out,
        preferred_element_type=jnp.float32,
    )
    attn_part = jnp.dot(to_request, slot_part, precision=lax.Precision.HIGHEST)
    up_partial = jnp.dot(mlp_in, w_up, preferred_element_type=jnp.float32)
    up = lax.psum(up_partial, "gx") + b_up
    hidden = jax.nn.gelu(up, approximate=False).astype(jnp.bfloat16)
    mlp_part = jnp.dot(hidden, w_down, preferred_element_type=jnp.float32)
    branches = lax.psum(attn_part + mlp_part, "gy")
    hidden_out = (wide_in + branches + b_out + b_down).astype(jnp.bfloat16)
    return (hidden_out, new_keys, new_values)


def solution(mesh):
    return jax.shard_map(
        on_device,
        mesh=mesh,
        in_specs=(
            P(None, "gx"),
            P("gx"),
            P("gx"),
            P("gx"),
            P("gx"),
            P("gx", "gy"),
            P("gy"),
            P("gy", "gx"),
            P("gx"),
            P("gx", "gy"),
            P("gy"),
            P("gy", "gx"),
            P("gx"),
            P("gx", "gy", None, None),
            P("gx", "gy", None, None),
            P(),
            P(),
        ),
        out_specs=(P(None, "gx"), P("gx", "gy", None, None), P("gx", "gy", None, None)),
        check_vma=False,
    )
```

profile of v0, /device:TPU:2, one launch (start us, length us, event | category | flops | bytes accessed | tf_op | source)
XLA Modules:
  0.0 324.9 jit_solution(3638242814341928627)
XLA Ops:
  7.2 0.0 copy-start
  7.2 0.0 copy-start.3
  7.2 0.0 all-reduce.5.cloned.1.call-start
  7.2 1.8 copy-done.3
  9.0 0.0 copy-start.9
  9.0 0.0 copy-start.10
  9.0 1.5 copy.66
  10.5 0.0 copy-done.4
  10.5 0.1 convert_reduce_fusion
  10.7 73.7 %all-reduce.1 = (f32[64]{0:T(128)S(1)}, f32[64]{0:T(128)S(1)}) all-reduce(f32[64]{0:T(128)S(1)} %get-tuple-element.4, f32[64]{0:T(128)S(1)} %get-tuple-element.3), channel_id=1, replica_groups=mesh['gx'=32,'gy'=8] {'gx'}, use_global_device_ids=true, to_apply=%region_4.5 | all-reduce | flops 128 | bytes 1024 | tf_op jit(solution)/shard_map/psum | solution.py:62
  84.4 1.2 fusion.61
  85.5 0.0 copy-done.10
  85.5 2.5 fusion.4
  88.0 0.0 all-reduce.5.cloned.1.call-update
  88.1 0.0 copy-done.13
  88.1 0.1 select_reduce_fusion
  88.2 0.1 fusion.118
  88.3 0.6 fusion.122
  91.5 0.6 dynamic-slice
  94.1 0.1 multiply_cosine_fusion
  94.2 0.1 iota_compare_fusion.4
  94.3 142.2 %all-reduce.5.cloned.1.call-done = (f32[64,1920]{1,0:T(8,128)}, f32[64,2560]{1,0:T(8,128)}) async-done(((f32[64,1920]{1,0:T(8,128)}, f32[64,2560]{1,0:T(8,128)}), (f32[64,1920]{1,0:T(8,128)}, f32[64,2560]{1,0:T(8,128)})) %all-reduce.5.cloned.1.call-update) | async-done | bytes 1146896
  236.5 0.8 dynamic-slice_add_fusion
  237.4 0.1 slice.90
  237.5 0.1 slice.91
  237.5 0.1 subtract_convert_fusion.1
  237.6 0.1 pad_maximum_fusion
  237.7 1.3 dynamic_update_slice.12
  239.1 0.1 maximum_bitcast_fusion
  239.1 1.3 dynamic_update_slice.13
  240.5 2.5 fusion.84
  243.0 0.1 fusion.3
  243.1 0.1 fusion.119
  243.2 0.1 copy.42
  243.3 0.0 copy-done.2
  243.4 0.0 copy-start.1
  243.4 0.4 fusion.59
  243.8 0.1 fusion.83
  243.9 0.9 reshape.113
  244.8 41.8 %all-gather = bf16[32,2,640]{2,1,0:T(2,128)(2,1)S(1)} all-gather(bf16[1,2,640]{2,1,0:T(2,128)(2,1)} %reshape.113), channel_id=1, replica_groups=mesh['gx'=32,'gy'=8] {'gx'}, dimensions={0}, use_global_device_ids=true | all-gather | bytes 84480 | tf_op jit(solution)/shard_map/all_gather | solution.py:117
  286.6 0.7 reshape.114
  287.3 1.1 fusion.123
  288.5 0.9 fusion.77
  289.3 0.0 copy-start.11
  289.4 0.0 copy-start.12
  289.4 3.5 %convolution_add_fusion = f32[64,160]{1,0:T(8,128)} fusion(f32[64,160]{1,0:T(8,128)S(1)} %fusion.77, bf16[2560,160]{0,1:T(8,128)(2,1)} %param.28, f32[64,2560]{1,0:T(8,128)} %get-tuple-element.8, f32[2560]{0:T(1024)} %param.27), kind=kOutput, calls=%fused_computation.1 | convolution fusion | flops 63252480 | bytes 1566720 | tf_op jit(solution)/shard_map/dot_general | solution.py:125
  292.9 24.5 %psum.31 = f32[64,160]{1,0:T(8,128)S(1)} all-reduce(f32[64,160]{1,0:T(8,128)} %convolution_add_fusion), channel_id=1, replica_groups=mesh['gx'=32,'gy'=8] {'gy'}, use_global_device_ids=true, to_apply=%region_9.10 | all-reduce | flops 10240 | bytes 81920 | tf_op jit(solution)/shard_map/psum | solution.py:126
  317.4 0.6 fusion.57
  (29 shorter events, 0.2 us)
Async XLA Ops:
  7.2 77.2 %copy-start = (bf16[160,2560]{1,0:T(8,128)(2,1)S(1)}, bf16[160,2560]{1,0:T(8,128)(2,1)}, u32[]{:S(2)}) copy-start(bf16[160,2560]{1,0:T(8,128)(2,1)} %param.26) | copy-start | bytes 2457604
  7.2 1.8 copy-start.3
  7.2 229.3 %all-reduce.5.cloned.1.call-start = ((), (), s32[]{:S(2)}) async-start(), calls=%async_computation | async-start | bytes 2293760
  9.0 1.5 copy-start.4
  9.0 75.4 %copy-start.7 = (f32[160]{0:T(256)S(1)}, f32[160]{0:T(256)}, u32[]{:S(2)}) copy-start(f32[160]{0:T(256)} %param.21) | copy-start | bytes 1924
  9.0 75.4 %copy-start.8 = (f32[160]{0:T(256)S(1)}, f32[160]{0:T(256)}, u32[]{:S(2)}) copy-start(f32[160]{0:T(256)} %param.20) | copy-start | bytes 1924
  9.0 76.5 %copy-start.6 = (s32[64]{0:T(128)S(1)}, s32[64]{0:T(128)}, u32[]{:S(2)}) copy-start(s32[64]{0:T(128)} %param.33) | copy-start | bytes 772
  9.0 76.5 %copy-start.9 = (f32[160]{0:T(256)S(1)}, f32[160]{0:T(256)}, u32[]{:S(2)}) copy-start(f32[160]{0:T(256)} %param.19) | copy-start | bytes 1924
  9.0 76.5 %copy-start.10 = (f32[160]{0:T(256)S(1)}, f32[160]{0:T(256)}, u32[]{:S(2)}) copy-start(f32[160]{0:T(256)} %param.18) | copy-start | bytes 1924
  10.5 77.6 %copy-start.13 = (s32[64]{0:T(128)S(1)}, s32[64]{0:T(128)}, u32[]{:S(2)}) copy-start(s32[64]{0:T(128)} %param.32) | copy-start | bytes 772
  10.5 81.0 %copy-start.14 = (u32[256]{0:T(256)S(1)}, u32[256]{0:T(256)}, u32[]{:S(2)}) copy-start(u32[256]{0:T(256)} %constant.103) | copy-start | bytes 3076
  10.5 225.9 %copy-start.5 = (f32[1920]{0:T(1024)S(1)}, f32[1920]{0:T(1024)}, u32[]{:S(2)}) copy-start(f32[1920]{0:T(1024)} %param.23) | copy-start | bytes 23044
  85.5 157.8 %copy-start.2 = (bf16[2,5,1024,128]{3,2,1,0:T(8,128)(2,1)S(1)}, bf16[2,5,1024,128]{3,2,1,0:T(8,128)(2,1)}, u32[]{:S(2)}) copy-start(bf16[2,5,1024,128]{3,2,1,0:T(8,128)(2,1)} %param.31) | copy-start | bytes 7864324
  243.4 49.5 %copy-start.1 = (bf16[2,5,1024,128]{3,2,1,0:T(8,128)(2,1)}, bf16[2,5,1024,128]{3,2,1,0:T(8,128)(2,1)S(1)}, u32[]{:S(2)}) copy-start(bf16[2,5,1024,128]{3,2,1,0:T(8,128)(2,1)S(1)} %dynamic_update_slice.15) | copy-start | bytes 7864324
  289.3 28.1 %copy-start.11 = (f32[160]{0:T(256)S(1)}, f32[160]{0:T(256)}, u32[]{:S(2)}) copy-start(f32[160]{0:T(256)} %param.29) | copy-start | bytes 1924
  289.4 28.1 %copy-start.12 = (f32[160]{0:T(256)S(1)}, f32[160]{0:T(256)}, u32[]{:S(2)}) copy-start(f32[160]{0:T(256)} %param.25) | copy-start | bytes 1924
Sparse Core Ops, SparseCore 0:
  88.2 148.2 all-reduce.4
where the time goes:
time: 325 us
  waiting for transfers between devices  142 us (44%)
  blocking collectives  140 us (43%)
  between operations  18.9 us (6%)
  matrix products  12.2 us (4%)
  local copies, waits for them, and re-layouts  9.11 us (3%)
    unnamed x2, waiting for transfers between devices  142 us
    psum x1, blocking collectives, on_device(): lax.psum((jnp.sum(wide_in, axis=1), jnp.sum(wide_in * wide_in, axis=1)),...  73.7 us
    all_gather x1, blocking collectives, on_device(): lax.all_gather(attended, 'gx', axis=0, tiled=True)  41.8 us
    psum x1, blocking collectives, on_device(): branches = lax.psum(attn_part + mlp_part, 'gy')  24.5 us
  transfers between devices with their start and end apart: 1, of which 1 were waited for; matrix products, arithmetic and copies ran while one was open for 0% of the time, Pallas kernels for 0%

commit v1 on v0

--- a/solution.py
+++ b/solution.py
@@ -113,11 +113,14 @@
         "shp,shpd->shd", weights_low, new_values, preferred_element_type=jnp.float32
     )
     attended = (weighted / total[:, :, None]).astype(jnp.bfloat16).reshape(rows_dev, heads_dev * HD)
-    slot_part = jnp.dot(
-        lax.all_gather(attended, "gx", axis=0, tiled=True),
-        w_out,
-        preferred_element_type=jnp.float32,
-    )
+
+    def roads_finish(u):
+        big = jnp.concatenate(
+            lax.all_to_all(jnp.stack([u] * lax.axis_size("gx")), "gx", 0, 0), axis=0
+        )
+        return big
+
+    slot_part = jnp.dot(roads_finish(attended), w_out, preferred_element_type=jnp.float32)
     attn_part = jnp.dot(to_request, slot_part, precision=lax.Precision.HIGHEST)
     up_partial = jnp.dot(mlp_in, w_up, preferred_element_type=jnp.float32)
     up = lax.psum(up_partial, "gx") + b_up

time: 325 us -> 299 us (0.920)
  blocking collectives: 140 us -> 114 us
    all_gather x1 -> x0, blocking collectives: 41.8 us -> none  [on_device(): lax.all_gather(attended, 'gx', axis=0, tiled=True)]
    all_to_all x0 -> x1, blocking collectives: none -> 16 us  [roads_finish(): lax.all_to_all(jnp.stack([u] * lax.axis_size('gx')), 'gx', 0, 0)]
  transfers between devices with their start and end apart: 1 -> 1, of which waited for: 1 -> 1; matrix products, arithmetic and copies ran while one was open for 0% -> 1% of each run, Pallas kernels for 0% -> 0%
where the time goes in v1:
time: 299 us; the launch traced here: 298 us
  waiting for transfers between devices  142 us (47%)
  blocking collectives  114 us (38%)
  between operations  18.9 us (6%)
  matrix products  12.2 us (4%)
  local copies, waits for them, and re-layouts  8.26 us (3%)
    unnamed x2, waiting for transfers between devices  142 us
    psum x1, blocking collectives, on_device(): lax.psum((jnp.sum(wide_in, axis=1), jnp.sum(wide_in * wide_in, axis=1)),...  73.7 us
    psum x1, blocking collectives, on_device(): branches = lax.psum(attn_part + mlp_part, 'gy')  24.5 us
    all_to_all x1, blocking collectives, roads_finish(): lax.all_to_all(jnp.stack([u] * lax.axis_size('gx')), 'gx', 0, 0)  16 us
  transfers between devices with their start and end apart: 1, of which 1 were waited for; matrix products, arithmetic and copies ran while one was open for 1% of the time, Pallas kernels for 0%

profile of v1, /device:TPU:2, one launch (start us, length us, event | category | flops | bytes accessed | tf_op | source)
XLA Modules:
  0.0 298.2 jit_solution(8507129718702844701)
XLA Ops:
  7.2 0.0 copy-start
  7.2 0.0 copy-start.3
  7.2 0.0 all-reduce.5.cloned.1.call-start
  7.2 1.8 copy-done.3
  9.0 0.0 copy-start.9
  9.0 0.0 copy-start.10
  9.0 1.5 copy.71
  10.5 0.0 copy-done.4
  10.5 0.1 convert_reduce_fusion
  10.7 73.7 %all-reduce.1 = (f32[64]{0:T(128)S(1)}, f32[64]{0:T(128)S(1)}) all-reduce(f32[64]{0:T(128)S(1)} %get-tuple-element.4, f32[64]{0:T(128)S(1)} %get-tuple-element.3), channel_id=1, replica_groups=mesh['gx'=32,'gy'=8] {'gx'}, use_global_device_ids=true, to_apply=%region_4.5 | all-reduce | flops 128 | bytes 1024 | tf_op jit(solution)/shard_map/psum | solution.py:62
  84.4 0.0 copy-done
  84.4 1.2 fusion.61
  85.5 0.0 copy-done.10
  85.5 2.5 fusion.4
  88.0 0.0 all-reduce.5.cloned.1.call-update
  88.1 0.0 copy-done.13
  88.1 0.1 select_reduce_fusion
  88.2 0.1 broadcast_add_fusion
  88.3 0.6 fusion.122
  91.5 0.6 dynamic-slice
  94.1 0.1 multiply_cosine_fusion
  94.2 0.1 iota_compare_fusion.4
  94.3 142.2 %all-reduce.5.cloned.1.call-done = (f32[64,1920]{1,0:T(8,128)}, f32[64,2560]{1,0:T(8,128)}) async-done(((f32[64,1920]{1,0:T(8,128)}, f32[64,2560]{1,0:T(8,128)}), (f32[64,1920]{1,0:T(8,128)}, f32[64,2560]{1,0:T(8,128)})) %all-reduce.5.cloned.1.call-update) | async-done | bytes 1146896
  236.5 0.8 dynamic-slice_add_fusion
  237.4 0.1 slice.91
  237.5 0.1 slice.90
  237.5 0.1 subtract_convert_fusion.1
  237.6 0.1 pad_maximum_fusion
  237.7 0.1 maximum_bitcast_fusion
  237.8 1.3 dynamic_update_slice.12
  239.1 1.3 dynamic_update_slice.13
  240.5 2.5 fusion.84
  243.0 0.1 fusion.3
  243.1 0.1 convert_bitcast_fusion
  243.2 0.1 copy.42
  243.4 0.0 copy-start.1
  243.4 0.4 fusion.59
  243.8 0.1 fusion.86
  243.9 0.1 stack.3
  244.0 16.0 %all_to_all.5 = bf16[32,2,640]{2,1,0:T(2,128)(2,1)S(1)} all-to-all(bf16[32,2,640]{2,1,0:T(2,128)(2,1)S(1)} %stack.3), channel_id=1, replica_groups=mesh['gx'=32,'gy'=8] {'gx'}, dimensions={0} | all-to-all | bytes 163840 | tf_op jit(solution)/shard_map/all_to_all | solution.py:119
  259.9 0.7 reshape.114
  260.6 1.2 fusion.123
  261.8 0.9 fusion.77
  262.7 0.0 copy-start.11
  262.7 0.0 copy-start.12
  262.7 3.5 %convolution_add_fusion = f32[64,160]{1,0:T(8,128)} fusion(f32[64,160]{1,0:T(8,128)S(1)} %fusion.77, bf16[2560,160]{0,1:T(8,128)(2,1)} %param.28, f32[64,2560]{1,0:T(8,128)} %get-tuple-element.8, f32[2560]{0:T(1024)} %param.27), kind=kOutput, calls=%fused_computation.1 | convolution fusion | flops 63252480 | bytes 1566720 | tf_op jit(solution)/shard_map/dot_general | solution.py:128
  266.3 24.5 %psum.31 = f32[64,160]{1,0:T(8,128)S(1)} all-reduce(f32[64,160]{1,0:T(8,128)} %convolution_add_fusion), channel_id=1, replica_groups=mesh['gx'=32,'gy'=8] {'gy'}, use_global_device_ids=true, to_apply=%region_9.10 | all-reduce | flops 10240 | bytes 81920 | tf_op jit(solution)/shard_map/psum | solution.py:129
  290.8 0.6 fusion.57
  (30 shorter events, 0.2 us)
Async XLA Ops:
  7.2 77.2 %copy-start = (bf16[160,2560]{1,0:T(8,128)(2,1)S(1)}, bf16[160,2560]{1,0:T(8,128)(2,1)}, u32[]{:S(2)}) copy-start(bf16[160,2560]{1,0:T(8,128)(2,1)} %param.26) | copy-start | bytes 2457604
  7.2 1.8 copy-start.3
  7.2 229.3 %all-reduce.5.cloned.1.call-start = ((), (), s32[]{:S(2)}) async-start(), calls=%async_computation.1 | async-start | bytes 2293760
  9.0 1.5 copy-start.4
  9.0 75.4 %copy-start.7 = (f32[160]{0:T(256)S(1)}, f32[160]{0:T(256)}, u32[]{:S(2)}) copy-start(f32[160]{0:T(256)} %param.21) | copy-start | bytes 1924
  9.0 75.4 %copy-start.8 = (f32[160]{0:T(256)S(1)}, f32[160]{0:T(256)}, u32[]{:S(2)}) copy-start(f32[160]{0:T(256)} %param.20) | copy-start | bytes 1924
  9.0 76.5 %copy-start.6 = (s32[64]{0:T(128)S(1)}, s32[64]{0:T(128)}, u32[]{:S(2)}) copy-start(s32[64]{0:T(128)} %param.33) | copy-start | bytes 772
  9.0 76.5 %copy-start.9 = (f32[160]{0:T(256)S(1)}, f32[160]{0:T(256)}, u32[]{:S(2)}) copy-start(f32[160]{0:T(256)} %param.19) | copy-start | bytes 1924
  9.0 76.5 %copy-start.10 = (f32[160]{0:T(256)S(1)}, f32[160]{0:T(256)}, u32[]{:S(2)}) copy-start(f32[160]{0:T(256)} %param.18) | copy-start | bytes 1924
  10.5 77.6 %copy-start.13 = (s32[64]{0:T(128)S(1)}, s32[64]{0:T(128)}, u32[]{:S(2)}) copy-start(s32[64]{0:T(128)} %param.32) | copy-start | bytes 772
  10.5 81.0 %copy-start.14 = (u32[256]{0:T(256)S(1)}, u32[256]{0:T(256)}, u32[]{:S(2)}) copy-start(u32[256]{0:T(256)} %constant.103) | copy-start | bytes 3076
  10.5 225.9 %copy-start.5 = (f32[1920]{0:T(1024)S(1)}, f32[1920]{0:T(1024)}, u32[]{:S(2)}) copy-start(f32[1920]{0:T(1024)} %param.23) | copy-start | bytes 23044
  85.5 157.8 %copy-start.2 = (bf16[2,5,1024,128]{3,2,1,0:T(8,128)(2,1)S(1)}, bf16[2,5,1024,128]{3,2,1,0:T(8,128)(2,1)}, u32[]{:S(2)}) copy-start(bf16[2,5,1024,128]{3,2,1,0:T(8,128)(2,1)} %param.31) | copy-start | bytes 7864324
  243.4 22.9 %copy-start.1 = (bf16[2,5,1024,128]{3,2,1,0:T(8,128)(2,1)}, bf16[2,5,1024,128]{3,2,1,0:T(8,128)(2,1)S(1)}, u32[]{:S(2)}) copy-start(bf16[2,5,1024,128]{3,2,1,0:T(8,128)(2,1)S(1)} %dynamic_update_slice.15) | copy-start | bytes 7864324
  262.7 28.1 %copy-start.11 = (f32[160]{0:T(256)S(1)}, f32[160]{0:T(256)}, u32[]{:S(2)}) copy-start(f32[160]{0:T(256)} %param.29) | copy-start | bytes 1924
  262.7 28.1 %copy-start.12 = (f32[160]{0:T(256)S(1)}, f32[160]{0:T(256)}, u32[]{:S(2)}) copy-start(f32[160]{0:T(256)} %param.25) | copy-start | bytes 1924
Sparse Core Ops, SparseCore 0:
  88.2 148.2 all-reduce.4
